TPU v7x, 256 devices: a whole 4x4x8 slice. The times are simulated.
256 devices in a mesh: row: 8 (over x, core), col: 32 (over y, z).
Axes of the slice: x: 4, y: 4, z: 8, core: 2. Of those that a mesh axis runs over, the one named last changes fastest.
Arguments:
- tokens: bfloat16 [1024, 6144], P('col', 'row'), may hold values from -6 to 6
- w_up: bfloat16 [6144, 24576], P('row', 'col'), may hold values from -0.078125 to 0.078125
- w_down: bfloat16 [24576, 6144], P('col', 'row'), may hold values from -0.0390625 to 0.0390625
- expert_in: bfloat16 [6144, 8192], P(None, 'col'), may hold values from -0.078125 to 0.078125
- expert_out: bfloat16 [8192, 6144], P('col'), may hold values from -0.125 to 0.125
- expert_ids: int32 [1024, 2], P('col'), may hold values from 0 to 3, as said below
- route_weights: bfloat16 [1024, 2], P('col'), may hold values from 0.25 to 1
- out_grad: bfloat16 [1024, 6144], P('col', 'row'), may hold values from -6 to 6
Outputs:
- layer_out: bfloat16 [1024, 6144], P('col', 'row')
- tokens_grad: bfloat16 [1024, 6144], P('col', 'row')
- up_grad: bfloat16 [6144, 24576], P('row', 'col')
- down_grad: bfloat16 [24576, 6144], P('col', 'row')
- expert_in_grad: bfloat16 [6144, 8192], P('row', 'col')
- expert_out_grad: bfloat16 [8192, 6144], P('col', 'row')
Inputs may be any that keep to these rules, and one draw needn't show every extreme that they name: `expert_ids`: the two experts of a token differ. In every aligned block of 4 tokens no expert is named by more than 3 of the block's pairs; one expert is named by exactly 3 pairs, the same expert in all blocks whose index leaves the same remainder modulo 32 // 4; the other experts' counts in a block differ by at most one. Every expert is named somewhere.
All inputs are finite; a program needn't handle non-finite values.
Results may differ from a plain program's by a relative error of at most 0.025.
Values may be sent and summed in bfloat16 or wider, within the bound.
No kernel may reach another device: no remote copies, remote signals or barrier semaphores. Data moves between devices by JAX's collectives and lax.ppermute only.
A program may use at most 128 MiB of HBM per device.

v0:
```python
import jax
import jax.numpy as jnp
from jax import lax
from jax.sharding import PartitionSpec as P

EXPERTS = 4
gelu_scale = 0.7978845608028654
gelu_cubic = 0.044715


def gelu_tanh(value):
    return 0.5 * value * (1.0 + jnp.tanh(gelu_scale * (value + gelu_cubic * value * value * value)))


def gelu_slope(value):
    inner = jnp.tanh(gelu_scale * (value + gelu_cubic * value * value * value))
    return 0.5 * (1.0 + inner) + 0.5 * value * (1.0 - inner * inner) * gelu_scale * (
        1.0 + 3.0 * gelu_cubic * value * value
    )


def slot_ranks(pairs):
    count = pairs.shape[-1]
    positions = jnp.arange(count, dtype=jnp.int32)
    earlier = positions[:, None] > positions[None, :]
    matching = pairs[..., :, None] == pairs[..., None, :]
    return jnp.sum((matching & earlier).astype(jnp.int32), axis=-1)


def on_device(tokens, w_up, w_down, expert_in, expert_out, expert_ids, route_weights, out_grad):
    row_count = lax.axis_size("row")
    col_count = lax.axis_size("col")
    tok_col = tokens.shape[0]
    block_len = tok_col // row_count
    group_len = col_count // EXPERTS
    slot_cap = max(2, 3 * block_len // 4)
    model_width = expert_out.shape[1]
    my_row = lax.axis_index("row")
    tok_panel = lax.all_gather(tokens, "col", axis=0, tiled=True)
    up_terms = jnp.dot(tok_panel, w_up, preferred_element_type=jnp.float32)
    preact = lax.psum_scatter(
        up_terms.astype(jnp.bfloat16), "row", scatter_dimension=0, tiled=True
    ).astype(jnp.float32)
    hidden_full = lax.all_gather(gelu_tanh(preact).astype(jnp.bfloat16), "row", axis=0, tiled=True)
    rows_in = hidden_full
    dense_term = lax.psum_scatter(
        jnp.dot(rows_in, w_down, preferred_element_type=jnp.float32).astype(jnp.bfloat16),
        "col",
        scatter_dimension=0,
        tiled=True,
    ).astype(jnp.float32)
    mixed_act = (tokens.astype(jnp.float32) + dense_term).astype(jnp.bfloat16)
    own_rows, own_grad = (
        lax.all_to_all(mixed_act, "row", split_axis=0, concat_axis=1, tiled=True),
        lax.all_to_all(out_grad, "row", split_axis=0, concat_axis=1, tiled=True),
    )
    chosen = lax.dynamic_slice_in_dim(expert_ids, my_row * block_len, block_len, 0).reshape(-1)
    weights_own = lax.dynamic_slice_in_dim(route_weights, my_row * block_len, block_len, 0)
    weights_flat = weights_own.reshape(-1).astype(jnp.float32)
    rows_x = jnp.repeat(own_rows, 2, axis=0)
    scaled = (weights_flat[:, None] * jnp.repeat(own_grad, 2, axis=0).astype(jnp.float32)).astype(
        jnp.bfloat16
    )
    slot_range = jnp.arange(slot_cap, dtype=jnp.int32)
    placed = slot_ranks(chosen)
    expert_range = jnp.arange(EXPERTS, dtype=jnp.int32)
    onehot = (
        (chosen[None, None, :] == expert_range[:, None, None])
        & (placed[None, None, :] == slot_range[None, :, None])
    ).astype(jnp.bfloat16)
    send_x = jnp.einsum("eca,ad->ecd", onehot, rows_x, preferred_element_type=jnp.float32).astype(
        jnp.bfloat16
    )
    send_g = jnp.einsum("eca,ad->ecd", onehot, scaled, preferred_element_type=jnp.float32).astype(
        jnp.bfloat16
    )
    send_x = jnp.repeat(send_x, group_len, axis=0)
    send_g = jnp.repeat(send_g, group_len, axis=0)
    got_x, got_g = (
        lax.all_to_all(send_x, "col", split_axis=0, concat_axis=0, tiled=True),
        lax.all_to_all(send_g, "col", split_axis=0, concat_axis=0, tiled=True),
    )
    inputs = got_x.reshape(-1, model_width)
    grads = got_g.reshape(-1, model_width)
    e_pre = jnp.dot(inputs, expert_in, preferred_element_type=jnp.float32)
    e_hidden = gelu_tanh(e_pre).astype(jnp.bfloat16)
    values = jnp.dot(e_hidden, expert_out, preferred_element_type=jnp.float32)
    e_dpre = (
        jnp.dot(grads, expert_out.T, preferred_element_type=jnp.float32) * gelu_slope(e_pre)
    ).astype(jnp.bfloat16)
    returns = jnp.dot(e_dpre, expert_in.T, preferred_element_type=jnp.float32)
    grad_in = jnp.dot(inputs.T, e_dpre, preferred_element_type=jnp.float32)
    grad_out = jnp.dot(e_hidden.T, grads, preferred_element_type=jnp.float32)
    values, returns, grad_in, grad_out = (values, returns, grad_in, grad_out)
    back_v, back_d = (
        lax.all_to_all(
            values.reshape(col_count, slot_cap, model_width).astype(jnp.bfloat16),
            "col",
            split_axis=0,
            concat_axis=0,
            tiled=True,
        ).astype(jnp.float32),
        lax.all_to_all(
            returns.reshape(col_count, slot_cap, model_width).astype(jnp.bfloat16),
            "col",
            split_axis=0,
            concat_axis=0,
            tiled=True,
        ).astype(jnp.float32),
    )
    flat_v = (
        back_v.reshape(EXPERTS, group_len, slot_cap, model_width)
        .sum(axis=1)
        .reshape(EXPERTS * slot_cap, model_width)
    )
    flat_d = (
        back_d.reshape(EXPERTS, group_len, slot_cap, model_width)
        .sum(axis=1)
        .reshape(EXPERTS * slot_cap, model_width)
    )
    lookup = chosen * slot_cap + placed
    moe_sum = (
        (weights_flat[:, None] * jnp.take(flat_v, lookup, axis=0))
        .reshape(block_len, 2, model_width)
        .sum(axis=1)
    )
    grad_sum = jnp.take(flat_d, lookup, axis=0).reshape(block_len, 2, model_width).sum(axis=1)
    layer_rows = (own_rows.astype(jnp.float32) + moe_sum).astype(jnp.bfloat16)
    grad_rows = (own_grad.astype(jnp.float32) + grad_sum).astype(jnp.bfloat16)
    layer_out, mixed_grad = (
        lax.all_to_all(layer_rows, "row", split_axis=1, concat_axis=0, tiled=True),
        lax.all_to_all(grad_rows, "row", split_axis=1, concat_axis=0, tiled=True),
    )
    expert_in_grad = lax.psum_scatter(
        grad_in.astype(jnp.bfloat16), "row", scatter_dimension=0, tiled=True
    )
    expert_out_grad = lax.psum_scatter(
        grad_out.astype(jnp.bfloat16), "row", scatter_dimension=1, tiled=True
    )
    cot_panel = lax.all_gather(mixed_grad, "col", axis=0, tiled=True)
    hgrad_terms = jnp.dot(cot_panel, w_down.T, preferred_element_type=jnp.float32)
    down_grad = jnp.dot(hidden_full.T, cot_panel, preferred_element_type=jnp.float32).astype(
        jnp.bfloat16
    )
    hidden_grad = lax.psum_scatter(
        hgrad_terms.astype(jnp.bfloat16), "row", scatter_dimension=0, tiled=True
    ).astype(jnp.float32)
    dpre_full = lax.all_gather(
        (hidden_grad * gelu_slope(preact)).astype(jnp.bfloat16), "row", axis=0, tiled=True
    )
    up_grad = jnp.dot(tok_panel.T, dpre_full, preferred_element_type=jnp.float32).astype(
        jnp.bfloat16
    )
    rows_in = dpre_full
    input_term = lax.psum_scatter(
        jnp.dot(rows_in, w_up.T, preferred_element_type=jnp.float32).astype(jnp.bfloat16),
        "col",
        scatter_dimension=0,
        tiled=True,
    ).astype(jnp.float32)
    tokens_grad = (mixed_grad.astype(jnp.float32) + input_term).astype(jnp.bfloat16)
    return (layer_out, tokens_grad, up_grad, down_grad, expert_in_grad, expert_out_grad)


def solution(mesh):
    in_specs = (
        P("col", "row"),
        P("row", "col"),
        P("col", "row"),
        P(None, "col"),
        P("col", None),
        P("col", None),
        P("col", None),
        P("col", "row"),
    )
    out_specs = (
        P("col", "row"),
        P("col", "row"),
        P("row", "col"),
        P("col", "row"),
        P("row", "col"),
        P("col", "row"),
    )
    return jax.shard_map(
        on_device, mesh=mesh, in_specs=in_specs, out_specs=out_specs, check_vma=False
    )
```

profile of v0, /device:TPU:8, one launch (start us, length us, event | category | flops | bytes accessed | tf_op | source)
XLA Modules:
  0.0 1058.8 jit_solution(8834172341026235586)
XLA Ops:
  8.0 81.4 %all-gather.5.cloned.1.call-done = bf16[1024,768]{1,0:T(8,128)(2,1)} async-done(((bf16[32,768]{1,0:T(8,128)(2,1)}), bf16[1024,768]{1,0:T(8,128)(2,1)}) %all-gather.5.cloned.1.call-update) | async-done | bytes 1572880 | tf_op jit(solution)/shard_map/all_gather | solution.py:39
  89.4 4.3 convolution_convert_fusion.9
  93.8 34.1 %reduce-scatter.7.cloned.1.call-done = bf16[128,768]{1,0:T(8,128)(2,1)} async-done(((bf16[1024,768]{1,0:T(8,128)(2,1)}), bf16[128,768]{1,0:T(8,128)(2,1)}) %reduce-scatter.7.cloned.1.call-update) | async-done | bytes 196624 | tf_op jit(solution)/shard_map/reduce_scatter | solution.py:41
  129.6 26.3 %all-gather.7.cloned.1.call-done = bf16[1024,768]{1,0:T(8,128)(2,1)} async-done(((bf16[128,768]{1,0:T(8,128)(2,1)}), bf16[1024,768]{1,0:T(8,128)(2,1)}) %all-gather.7.cloned.1.call-update) | async-done | bytes 1572880 | tf_op jit(solution)/shard_map/all_gather | solution.py:44
  156.0 4.3 convolution_convert_fusion.8
  166.3 4.2 all-to-all-done.4
  171.4 207.3 %reduce-scatter.9.cloned.1.call-done = bf16[32,768]{1,0:T(8,128)(2,1)} async-done(((bf16[1024,768]{1,0:T(8,128)(2,1)}), bf16[32,768]{1,0:T(8,128)(2,1)}) %reduce-scatter.9.cloned.1.call-update) | async-done | bytes 49168 | tf_op jit(solution)/shard_map/reduce_scatter | solution.py:46
  380.1 4.2 all-to-all-start
  384.8 5.2 all-to-all-done
  391.9 8.0 all-to-all-start.5
  401.1 35.5 %all-to-all-done.5 = bf16[32,3,6144]{2,1,0:T(4,128)(2,1)} async-done(((bf16[32,3,6144]{2,1,0:T(4,128)(2,1)}), bf16[32,3,6144]{2,1,0:T(4,128)(2,1)}, u32[]{:S(2)}, u32[]{:S(2)}) %all-to-all-start.5) | async-done | bytes 1179680 | tf_op jit(solution)/shard_map/all_to_all | solution.py:81
  438.5 8.2 all-to-all-start.1
  446.7 4.0 reshape.146
  450.7 32.5 %all-to-all-done.1 = bf16[32,3,6144]{2,1,0:T(4,128)(2,1)} async-done(((bf16[32,3,6144]{2,1,0:T(4,128)(2,1)}), bf16[32,3,6144]{2,1,0:T(4,128)(2,1)}, u32[]{:S(2)}, u32[]{:S(2)}) %all-to-all-start.1) | async-done | bytes 1179680 | tf_op jit(solution)/shard_map/all_to_all | solution.py:80
  483.2 3.9 reshape.140
  497.3 8.1 all-to-all-start.6
  512.9 29.0 %all-to-all-done.6 = bf16[32,3,6144]{2,1,0:T(4,128)(2,1)} async-done(((bf16[32,3,6144]{2,1,0:T(4,128)(2,1)}), bf16[32,3,6144]{2,1,0:T(4,128)(2,1)}, u32[]{:S(2)}, u32[]{:S(2)}) %all-to-all-start.6) | async-done | bytes 1179680 | tf_op jit(solution)/shard_map/all_to_all | solution.py:103
  541.9 8.1 all-to-all-start.2
  554.4 32.1 %all-to-all-done.2 = bf16[32,3,6144]{2,1,0:T(4,128)(2,1)} async-done(((bf16[32,3,6144]{2,1,0:T(4,128)(2,1)}), bf16[32,3,6144]{2,1,0:T(4,128)(2,1)}, u32[]{:S(2)}, u32[]{:S(2)}) %all-to-all-start.2) | async-done | bytes 1179680 | tf_op jit(solution)/shard_map/all_to_all | solution.py:96
  599.5 7.9 all_to_all.84
  608.1 73.4 %all-gather.9.cloned.1.call-done = bf16[1024,768]{1,0:T(8,128)(2,1)} async-done(((bf16[32,768]{1,0:T(8,128)(2,1)}), bf16[1024,768]{1,0:T(8,128)(2,1)}) %all-gather.9.cloned.1.call-update) | async-done | bytes 1572880 | tf_op jit(solution)/shard_map/all_gather | solution.py:140
  681.5 4.3 convolution_convert_fusion.7
  685.9 34.2 %reduce-scatter.11.cloned.1.call-done = bf16[128,768]{1,0:T(8,128)(2,1)} async-done(((bf16[1024,768]{1,0:T(8,128)(2,1)}), bf16[128,768]{1,0:T(8,128)(2,1)}) %reduce-scatter.11.cloned.1.call-update) | async-done | bytes 196624 | tf_op jit(solution)/shard_map/reduce_scatter | solution.py:145
  722.1 26.1 %all-gather.11.cloned.1.call-done = bf16[1024,768]{1,0:T(8,128)(2,1)} async-done(((bf16[128,768]{1,0:T(8,128)(2,1)}), bf16[1024,768]{1,0:T(8,128)(2,1)}) %all-gather.11.cloned.1.call-update) | async-done | bytes 1572880 | tf_op jit(solution)/shard_map/all_gather | solution.py:148
  748.1 4.3 convolution_convert_fusion.6
  753.4 3.9 convolution_convert_fusion
  758.1 4.0 convolution_convert_fusion.1
  763.3 8.6 all_to_all.85
  772.5 4.5 convolution_convert_fusion.10
  781.8 188.9 %reduce-scatter.13.cloned.1.call-done = bf16[32,768]{1,0:T(8,128)(2,1)} async-done(((bf16[1024,768]{1,0:T(8,128)(2,1)}), bf16[32,768]{1,0:T(8,128)(2,1)}) %reduce-scatter.13.cloned.1.call-update) | async-done | bytes 49168 | tf_op jit(solution)/shard_map/reduce_scatter | solution.py:155
  972.2 39.5 %reduce-scatter.17.cloned.1.call-done = bf16[256,768]{1,0:T(8,128)(2,1)} async-done(((bf16[256,6144]{1,0:T(8,128)(2,1)}), bf16[256,768]{1,0:T(8,128)(2,1)}) %reduce-scatter.17.cloned.1.call-update) | async-done | bytes 393232 | tf_op jit(solution)/shard_map/reduce_scatter | solution.py:137
  1011.6 40.3 %reduce-scatter.15.cloned.1.call-done = bf16[768,256]{1,0:T(8,128)(2,1)} async-done(((bf16[6144,256]{1,0:T(8,128)(2,1)}), bf16[768,256]{1,0:T(8,128)(2,1)}) %reduce-scatter.15.cloned.1.call-update) | async-done | bytes 393232 | tf_op jit(solution)/shard_map/reduce_scatter | solution.py:134
  (108 shorter events, 63.7 us)
Async XLA Ops:
  7.2 479.9 %copy-start = (bf16[6144,256]{1,0:T(8,128)(2,1)S(1)}, bf16[6144,256]{1,0:T(8,128)(2,1)}, u32[]{:S(2)}) copy-start(bf16[6144,256]{1,0:T(8,128)(2,1)} %param.13) | copy-start | bytes 9437188
  7.2 82.2 %all-gather.5.cloned.1.call-start = ((), (), s32[]{:S(2)}) async-start(), calls=%async_computation.14 | async-start | bytes 1622016 | tf_op jit(solution)/shard_map/all_gather | solution.py:39
  7.9 119.9 %reduce-scatter.7.cloned.1.call-start = ((), (), s32[]{:S(2)}) async-start(), calls=%async_computation.15 | async-start | bytes 1769472 | tf_op jit(solution)/shard_map/reduce_scatter | solution.py:41
  93.7 62.3 %all-gather.7.cloned.1.call-start = ((), (), s32[]{:S(2)}) async-start(), calls=%async_computation.16 | async-start | bytes 1769472 | tf_op jit(solution)/shard_map/all_gather | solution.py:44
  129.6 249.0 %reduce-scatter.9.cloned.1.call-start = ((), (), s32[]{:S(2)}) async-start(), calls=%async_computation.17 | async-start | bytes 1622016 | tf_op jit(solution)/shard_map/reduce_scatter | solution.py:46
  160.3 0.8 copy-start.11
  160.3 4.8 copy-start.12
  160.3 5.8 copy-start.13
  161.7 8.8 all-to-all-start.4
  170.5 0.6 copy-start.10
  380.1 9.9 all-to-all-start
  391.9 44.8 %all-to-all-start.5 = ((bf16[32,3,6144]{2,1,0:T(4,128)(2,1)}), bf16[32,3,6144]{2,1,0:T(4,128)(2,1)}, u32[]{:S(2)}, u32[]{:S(2)}) async-start(bf16[32,3,6144]{2,1,0:T(4,128)(2,1)} %bitcast.50), calls=%async_computation.7 | async-start | bytes 3145728 | tf_op jit(solution)/shard_map/all_to_all | solution.py:81
  438.5 44.6 %all-to-all-start.1 = ((bf16[32,3,6144]{2,1,0:T(4,128)(2,1)}), bf16[32,3,6144]{2,1,0:T(4,128)(2,1)}, u32[]{:S(2)}, u32[]{:S(2)}) async-start(bf16[32,3,6144]{2,1,0:T(4,128)(2,1)} %bitcast.51), calls=%async_computation.3 | async-start | bytes 3145728 | tf_op jit(solution)/shard_map/all_to_all | solution.py:80
  487.1 2.2 copy-start.1
  487.1 2.6 copy-start.2
  489.7 15.8 %copy-start.3 = (f32[96,256]{1,0:T(8,128)}, f32[96,256]{1,0:T(8,128)S(1)}, u32[]{:S(2)}) copy-start(f32[96,256]{1,0:T(8,128)S(1)} %fusion.29) | copy-start | bytes 294916
  497.3 44.6 %all-to-all-start.6 = ((bf16[32,3,6144]{2,1,0:T(4,128)(2,1)}), bf16[32,3,6144]{2,1,0:T(4,128)(2,1)}, u32[]{:S(2)}, u32[]{:S(2)}) async-start(bf16[32,3,6144]{2,1,0:T(4,128)(2,1)} %convert_element_type.155), calls=%async_computation.8 | async-start | bytes 3145728 | tf_op jit(solution)/shard_map/all_to_all | solution.py:103
  512.8 37.4 %copy-start.15 = (s32[8]{0:T(128)S(1)}, s32[8]{0:T(128)}, u32[]{:S(2)}) copy-start(s32[8]{0:T(128)} %copy-done.14) | copy-start | bytes 100
  541.9 44.6 %all-to-all-start.2 = ((bf16[32,3,6144]{2,1,0:T(4,128)(2,1)}), bf16[32,3,6144]{2,1,0:T(4,128)(2,1)}, u32[]{:S(2)}, u32[]{:S(2)}) async-start(bf16[32,3,6144]{2,1,0:T(4,128)(2,1)} %convert_element_type.144), calls=%async_computation.4 | async-start | bytes 3145728 | tf_op jit(solution)/shard_map/all_to_all | solution.py:96
  550.0 131.5 %all-gather.9.cloned.1.call-start = ((), (), s32[]{:S(2)}) async-start(), calls=%async_computation.18 | async-start | bytes 1622016 | tf_op jit(solution)/shard_map/all_gather | solution.py:140
  592.5 2.4 copy-start.6
  608.1 112.0 %reduce-scatter.11.cloned.1.call-start = ((), (), s32[]{:S(2)}) async-start(), calls=%async_computation.19 | async-start | bytes 1769472 | tf_op jit(solution)/shard_map/reduce_scatter | solution.py:145
  685.9 34.2 %copy-start.5 = (bf16[128,768]{1,0:T(8,128)(2,1)S(1)}, bf16[128,768]{1,0:T(8,128)(2,1)}, u32[]{:S(2)}) copy-start(bf16[128,768]{1,0:T(8,128)(2,1)} %reduce-scatter.7.cloned.1.call-done) | copy-start | bytes 589828
  685.9 62.2 %all-gather.11.cloned.1.call-start = ((), (), s32[]{:S(2)}) async-start(), calls=%async_computation.20 | async-start | bytes 1769472 | tf_op jit(solution)/shard_map/all_gather | solution.py:148
  722.0 248.7 %reduce-scatter.13.cloned.1.call-start = ((), (), s32[]{:S(2)}) async-start(), calls=%async_computation.21 | async-start | bytes 1622016 | tf_op jit(solution)/shard_map/reduce_scatter | solution.py:155
  752.5 0.9 copy-start.4
  752.5 259.1 %reduce-scatter.17.cloned.1.call-start = ((), (), s32[]{:S(2)}) async-start(), calls=%async_computation.23 | async-start | bytes 3538944 | tf_op jit(solution)/shard_map/reduce_scatter | solution.py:137
  757.3 0.8 copy-start.8
  757.3 294.6 %reduce-scatter.15.cloned.1.call-start = ((), (), s32[]{:S(2)}) async-start(), calls=%async_computation.22 | async-start | bytes 3538944 | tf_op jit(solution)/shard_map/reduce_scatter | solution.py:134
  772.5 4.5 copy-start.16
  772.5 4.5 copy-start.17
  779.4 191.3 %copy-start.9 = (bf16[32,768]{1,0:T(8,128)(2,1)S(1)}, bf16[32,768]{1,0:T(8,128)(2,1)}, u32[]{:S(2)}) copy-start(bf16[32,768]{1,0:T(8,128)(2,1)} %all_to_all.75) | copy-start | bytes 147460
  (2 other events, 1.1 us)
Sparse Core Ops, SparseCore 0:
  10.6 78.7 all-gather.4
  93.8 33.9 reduce-scatter.6
  130.2 25.6 all-gather.6
  160.4 218.1 reduce-scatter.8
  608.2 73.2 all-gather.8
  686.0 34.0 reduce-scatter.10
  722.5 25.5 all-gather.10
  752.6 218.0 reduce-scatter.12
  973.9 37.7 reduce-scatter.16
  1014.6 37.3 reduce-scatter.14
where the time goes:
time: 1060 us
  waiting for transfers between devices  891 us (84%)
  matrix products  41.5 us (4%)
  starting transfers between devices  40.6 us (4%)
  local copies, waits for them, and re-layouts  38.4 us (4%)
  other arithmetic  16.7 us (2%)
  blocking collectives  16.5 us (2%)
  between operations  14.4 us (1%)
    reduce_scatter x1, waiting for transfers between devices, on_device(): lax.psum_scatter(jnp.dot(rows_in, w_down, preferred_element_type=jnp.floa...  207 us
    reduce_scatter x1, waiting for transfers between devices, on_device(): lax.psum_scatter(jnp.dot(rows_in, w_up.T, preferred_element_type=jnp.floa...  189 us
    all_gather x1, waiting for transfers between devices, on_device(): tok_panel = lax.all_gather(tokens, 'col', axis=0, tiled=True)  81.4 us
    all_gather x1, waiting for transfers between devices, on_device(): cot_panel = lax.all_gather(mixed_grad, 'col', axis=0, tiled=True)  73.4 us
    reduce_scatter x1, waiting for transfers between devices, on_device(): lax.psum_scatter(grad_in.astype(jnp.bfloat16), 'row', scatter_dimension=0...  40.3 us
    reduce_scatter x1, waiting for transfers between devices, on_device(): lax.psum_scatter(grad_out.astype(jnp.bfloat16), 'row', scatter_dimension=...  39.5 us
    all_to_all x1, waiting for transfers between devices, on_device(): lax.all_to_all(send_g, 'col', split_axis=0, concat_axis=0, tiled=True)  35.5 us
    reduce_scatter x1, waiting for transfers between devices, on_device(): lax.psum_scatter(hgrad_terms.astype(jnp.bfloat16), 'row', scatter_dimensi...  34.2 us
  transfers between devices with their start and end apart: 16, of which 16 were waited for; matrix products, arithmetic and copies ran while one was open for 4% of the time, Pallas kernels for 0%

commit v1 on v0

--- a/solution.py
+++ b/solution.py
@@ -145,8 +145,16 @@
     hidden_grad = lax.psum_scatter(
         hgrad_terms.astype(jnp.bfloat16), "row", scatter_dimension=0, tiled=True
     ).astype(jnp.float32)
-    dpre_full = lax.all_gather(
-        (hidden_grad * gelu_slope(preact)).astype(jnp.bfloat16), "row", axis=0, tiled=True
+    dpre_full = jnp.concatenate(
+        lax.all_to_all(
+            jnp.stack(
+                [(hidden_grad * gelu_slope(preact)).astype(jnp.bfloat16)] * lax.axis_size("row")
+            ),
+            "row",
+            0,
+            0,
+        ),
+        axis=0,
     )
     up_grad = jnp.dot(tok_panel.T, dpre_full, preferred_element_type=jnp.float32).astype(
         jnp.bfloat16

time: 1060 us -> 1060 us (level)
  waiting for transfers between devices: 891 us -> 865 us
  blocking collectives: 16.5 us -> 40 us
    all_gather x1 -> x0, waiting for transfers between devices: 26.1 us -> none  [on_device(): lax.all_gather((hidden_grad * gelu_slope(preact)).astype(jnp.bfloat16), '...]
    all_to_all x0 -> x1, blocking collectives: none -> 24.2 us  [on_device(): lax.all_to_all(jnp.stack([(hidden_grad * gelu_slope(preact)).astype(jnp.b...]
  transfers between devices with their start and end apart: 16 -> 15, of which waited for: 16 -> 15; matrix products, arithmetic and copies ran while one was open for 4% -> 4% of each run, Pallas kernels for 0% -> 0%
where the time goes in v1:
time: 1060 us; the launch traced here: 1050 us
  waiting for transfers between devices  865 us (82%)
  starting transfers between devices  40.6 us (4%)
  blocking collectives  40 us (4%)
  local copies, waits for them, and re-layouts  39.7 us (4%)
  matrix products  39.7 us (4%)
  other arithmetic  16 us (2%)
  between operations  14.1 us (1%)
    reduce_scatter x1, waiting for transfers between devices, on_device(): lax.psum_scatter(jnp.dot(rows_in, w_down, preferred_element_type=jnp.floa...  207 us
    reduce_scatter x1, waiting for transfers between devices, on_device(): lax.psum_scatter(jnp.dot(rows_in, w_up.T, preferred_element_type=jnp.floa...  189 us
    all_gather x1, waiting for transfers between devices, on_device(): tok_panel = lax.all_gather(tokens, 'col', axis=0, tiled=True)  81.4 us
    all_gather x1, waiting for transfers between devices, on_device(): cot_panel = lax.all_gather(mixed_grad, 'col', axis=0, tiled=True)  73.4 us
    reduce_scatter x1, waiting for transfers between devices, on_device(): lax.psum_scatter(grad_in.astype(jnp.bfloat16), 'row', scatter_dimension=0...  40.5 us
    reduce_scatter x1, waiting for transfers between devices, on_device(): lax.psum_scatter(grad_out.astype(jnp.bfloat16), 'row', scatter_dimension=...  39.3 us
    all_to_all x1, waiting for transfers between devices, on_device(): lax.all_to_all(send_g, 'col', split_axis=0, concat_axis=0, tiled=True)  35.5 us
    reduce_scatter x1, waiting for transfers between devices, on_device(): lax.psum_scatter(hgrad_terms.astype(jnp.bfloat16), 'row', scatter_dimensi...  34.1 us
  transfers between devices with their start and end apart: 15, of which 15 were waited for; matrix products, arithmetic and copies ran while one was open for 4% of the time, Pallas kernels for 0%

profile of v1, /device:TPU:8, one launch (start us, length us, event | category | flops | bytes accessed | tf_op | source)
XLA Modules:
  0.0 1054.7 jit_solution(16203622864471059967)
XLA Ops:
  8.0 81.4 %all-gather.4.cloned.1.call-done = bf16[1024,768]{1,0:T(8,128)(2,1)} async-done(((bf16[32,768]{1,0:T(8,128)(2,1)}), bf16[1024,768]{1,0:T(8,128)(2,1)}) %all-gather.4.cloned.1.call-update) | async-done | bytes 1572880 | tf_op jit(solution)/shard_map/all_gather | solution.py:39
  89.4 4.3 convolution_convert_fusion.9
  93.8 34.1 %reduce-scatter.7.cloned.1.call-done = bf16[128,768]{1,0:T(8,128)(2,1)} async-done(((bf16[1024,768]{1,0:T(8,128)(2,1)}), bf16[128,768]{1,0:T(8,128)(2,1)}) %reduce-scatter.7.cloned.1.call-update) | async-done | bytes 196624 | tf_op jit(solution)/shard_map/reduce_scatter | solution.py:41
  129.6 26.3 %all-gather.6.cloned.1.call-done = bf16[1024,768]{1,0:T(8,128)(2,1)} async-done(((bf16[128,768]{1,0:T(8,128)(2,1)}), bf16[1024,768]{1,0:T(8,128)(2,1)}) %all-gather.6.cloned.1.call-update) | async-done | bytes 1572880 | tf_op jit(solution)/shard_map/all_gather | solution.py:44
  156.0 4.3 convolution_convert_fusion.8
  166.3 4.2 all-to-all-done.4
  171.3 207.4 %reduce-scatter.9.cloned.1.call-done = bf16[32,768]{1,0:T(8,128)(2,1)} async-done(((bf16[1024,768]{1,0:T(8,128)(2,1)}), bf16[32,768]{1,0:T(8,128)(2,1)}) %reduce-scatter.9.cloned.1.call-update) | async-done | bytes 49168 | tf_op jit(solution)/shard_map/reduce_scatter | solution.py:46
  380.2 4.2 all-to-all-start
  384.8 5.2 all-to-all-done
  391.9 8.0 all-to-all-start.5
  401.2 35.5 %all-to-all-done.5 = bf16[32,3,6144]{2,1,0:T(4,128)(2,1)} async-done(((bf16[32,3,6144]{2,1,0:T(4,128)(2,1)}), bf16[32,3,6144]{2,1,0:T(4,128)(2,1)}, u32[]{:S(2)}, u32[]{:S(2)}) %all-to-all-start.5) | async-done | bytes 1179680 | tf_op jit(solution)/shard_map/all_to_all | solution.py:81
  438.6 8.2 all-to-all-start.1
  446.8 4.0 reshape.151
  450.8 32.5 %all-to-all-done.1 = bf16[32,3,6144]{2,1,0:T(4,128)(2,1)} async-done(((bf16[32,3,6144]{2,1,0:T(4,128)(2,1)}), bf16[32,3,6144]{2,1,0:T(4,128)(2,1)}, u32[]{:S(2)}, u32[]{:S(2)}) %all-to-all-start.1) | async-done | bytes 1179680 | tf_op jit(solution)/shard_map/all_to_all | solution.py:80
  483.2 3.9 reshape.145
  493.6 3.8 convert_element_type.155
  497.4 8.1 all-to-all-start.6
  513.0 29.0 %all-to-all-done.6 = bf16[32,3,6144]{2,1,0:T(4,128)(2,1)} async-done(((bf16[32,3,6144]{2,1,0:T(4,128)(2,1)}), bf16[32,3,6144]{2,1,0:T(4,128)(2,1)}, u32[]{:S(2)}, u32[]{:S(2)}) %all-to-all-start.6) | async-done | bytes 1179680 | tf_op jit(solution)/shard_map/all_to_all | solution.py:103
  542.0 8.1 all-to-all-start.2
  554.5 32.1 %all-to-all-done.2 = bf16[32,3,6144]{2,1,0:T(4,128)(2,1)} async-done(((bf16[32,3,6144]{2,1,0:T(4,128)(2,1)}), bf16[32,3,6144]{2,1,0:T(4,128)(2,1)}, u32[]{:S(2)}, u32[]{:S(2)}) %all-to-all-start.2) | async-done | bytes 1179680 | tf_op jit(solution)/shard_map/all_to_all | solution.py:96
  599.6 7.9 all_to_all.89
  608.3 73.4 %all-gather.8.cloned.1.call-done = bf16[1024,768]{1,0:T(8,128)(2,1)} async-done(((bf16[32,768]{1,0:T(8,128)(2,1)}), bf16[1024,768]{1,0:T(8,128)(2,1)}) %all-gather.8.cloned.1.call-update) | async-done | bytes 1572880 | tf_op jit(solution)/shard_map/all_gather | solution.py:140
  681.6 4.3 convolution_convert_fusion.7
  686.0 34.1 %reduce-scatter.11.cloned.1.call-done = bf16[128,768]{1,0:T(8,128)(2,1)} async-done(((bf16[1024,768]{1,0:T(8,128)(2,1)}), bf16[128,768]{1,0:T(8,128)(2,1)}) %reduce-scatter.11.cloned.1.call-update) | async-done | bytes 196624 | tf_op jit(solution)/shard_map/reduce_scatter | solution.py:145
  721.5 24.2 %all_to_all.90 = bf16[8,128,768]{2,1,0:T(8,128)(2,1)S(1)} all-to-all(bf16[8,128,768]{2,1,0:T(8,128)(2,1)S(1)} %stack.2), channel_id=1, replica_groups=mesh['row'=8,'col'=32] {'row'}, dimensions={0} | all-to-all | bytes 3145728 | tf_op jit(solution)/shard_map/all_to_all | solution.py:149
  750.3 3.9 convolution_convert_fusion
  755.0 4.0 convolution_convert_fusion.1
  760.2 7.9 all_to_all.91
  768.7 4.5 convolution_convert_fusion.10
  778.1 188.8 %reduce-scatter.13.cloned.1.call-done = bf16[32,768]{1,0:T(8,128)(2,1)} async-done(((bf16[1024,768]{1,0:T(8,128)(2,1)}), bf16[32,768]{1,0:T(8,128)(2,1)}) %reduce-scatter.13.cloned.1.call-update) | async-done | bytes 49168 | tf_op jit(solution)/shard_map/reduce_scatter | solution.py:163
  968.3 39.3 %reduce-scatter.17.cloned.1.call-done = bf16[256,768]{1,0:T(8,128)(2,1)} async-done(((bf16[256,6144]{1,0:T(8,128)(2,1)}), bf16[256,768]{1,0:T(8,128)(2,1)}) %reduce-scatter.17.cloned.1.call-update) | async-done | bytes 393232 | tf_op jit(solution)/shard_map/reduce_scatter | solution.py:137
  1007.6 40.5 %reduce-scatter.15.cloned.1.call-done = bf16[768,256]{1,0:T(8,128)(2,1)} async-done(((bf16[6144,256]{1,0:T(8,128)(2,1)}), bf16[768,256]{1,0:T(8,128)(2,1)}) %reduce-scatter.15.cloned.1.call-update) | async-done | bytes 393232 | tf_op jit(solution)/shard_map/reduce_scatter | solution.py:134
  (111 shorter events, 63.1 us)
Async XLA Ops:
  7.2 480.0 %copy-start = (bf16[6144,256]{1,0:T(8,128)(2,1)S(1)}, bf16[6144,256]{1,0:T(8,128)(2,1)}, u32[]{:S(2)}) copy-start(bf16[6144,256]{1,0:T(8,128)(2,1)} %param.13) | copy-start | bytes 9437188
  7.2 82.2 %all-gather.4.cloned.1.call-start = ((), (), s32[]{:S(2)}) async-start(), calls=%async_computation.15 | async-start | bytes 1622016 | tf_op jit(solution)/shard_map/all_gather | solution.py:39
  7.9 119.9 %reduce-scatter.7.cloned.1.call-start = ((), (), s32[]{:S(2)}) async-start(), calls=%async_computation.16 | async-start | bytes 1769472 | tf_op jit(solution)/shard_map/reduce_scatter | solution.py:41
  93.7 62.3 %all-gather.6.cloned.1.call-start = ((), (), s32[]{:S(2)}) async-start(), calls=%async_computation.17 | async-start | bytes 1769472 | tf_op jit(solution)/shard_map/all_gather | solution.py:44
  129.6 249.1 %reduce-scatter.9.cloned.1.call-start = ((), (), s32[]{:S(2)}) async-start(), calls=%async_computation.18 | async-start | bytes 1622016 | tf_op jit(solution)/shard_map/reduce_scatter | solution.py:46
  160.3 0.8 copy-start.13
  160.3 4.8 copy-start.14
  160.3 5.8 copy-start.15
  161.7 8.8 all-to-all-start.4
  380.2 9.9 all-to-all-start
  391.9 44.8 %all-to-all-start.5 = ((bf16[32,3,6144]{2,1,0:T(4,128)(2,1)}), bf16[32,3,6144]{2,1,0:T(4,128)(2,1)}, u32[]{:S(2)}, u32[]{:S(2)}) async-start(bf16[32,3,6144]{2,1,0:T(4,128)(2,1)} %bitcast.51), calls=%async_computation.7 | async-start | bytes 3145728 | tf_op jit(solution)/shard_map/all_to_all | solution.py:81
  438.6 44.6 %all-to-all-start.1 = ((bf16[32,3,6144]{2,1,0:T(4,128)(2,1)}), bf16[32,3,6144]{2,1,0:T(4,128)(2,1)}, u32[]{:S(2)}, u32[]{:S(2)}) async-start(bf16[32,3,6144]{2,1,0:T(4,128)(2,1)} %bitcast.52), calls=%async_computation.3 | async-start | bytes 3145728 | tf_op jit(solution)/shard_map/all_to_all | solution.py:80
  487.2 2.2 copy-start.1
  487.2 2.6 copy-start.2
  489.8 15.8 %copy-start.5 = (f32[96,256]{1,0:T(8,128)}, f32[96,256]{1,0:T(8,128)S(1)}, u32[]{:S(2)}) copy-start(f32[96,256]{1,0:T(8,128)S(1)} %fusion.29) | copy-start | bytes 294916
  497.4 44.6 %all-to-all-start.6 = ((bf16[32,3,6144]{2,1,0:T(4,128)(2,1)}), bf16[32,3,6144]{2,1,0:T(4,128)(2,1)}, u32[]{:S(2)}, u32[]{:S(2)}) async-start(bf16[32,3,6144]{2,1,0:T(4,128)(2,1)} %convert_element_type.155), calls=%async_computation.8 | async-start | bytes 3145728 | tf_op jit(solution)/shard_map/all_to_all | solution.py:103
  513.0 37.4 %copy-start.17 = (s32[8]{0:T(128)S(1)}, s32[8]{0:T(128)}, u32[]{:S(2)}) copy-start(s32[8]{0:T(128)} %copy-done.16) | copy-start | bytes 100
  542.0 44.6 %all-to-all-start.2 = ((bf16[32,3,6144]{2,1,0:T(4,128)(2,1)}), bf16[32,3,6144]{2,1,0:T(4,128)(2,1)}, u32[]{:S(2)}, u32[]{:S(2)}) async-start(bf16[32,3,6144]{2,1,0:T(4,128)(2,1)} %convert_element_type.144), calls=%async_computation.4 | async-start | bytes 3145728 | tf_op jit(solution)/shard_map/all_to_all | solution.py:96
  550.1 131.5 %all-gather.8.cloned.1.call-start = ((), (), s32[]{:S(2)}) async-start(), calls=%async_computation.19 | async-start | bytes 1622016 | tf_op jit(solution)/shard_map/all_gather | solution.py:140
  592.7 2.4 copy-start.8
  608.2 111.9 %reduce-scatter.11.cloned.1.call-start = ((), (), s32[]{:S(2)}) async-start(), calls=%async_computation.20 | async-start | bytes 1769472 | tf_op jit(solution)/shard_map/reduce_scatter | solution.py:145
  686.0 34.1 %copy-start.7 = (bf16[128,768]{1,0:T(8,128)(2,1)S(1)}, bf16[128,768]{1,0:T(8,128)(2,1)}, u32[]{:S(2)}) copy-start(bf16[128,768]{1,0:T(8,128)(2,1)} %reduce-scatter.7.cloned.1.call-done) | copy-start | bytes 589828
  686.0 280.9 %reduce-scatter.13.cloned.1.call-start = ((), (), s32[]{:S(2)}) async-start(), calls=%async_computation.21 | async-start | bytes 1622016 | tf_op jit(solution)/shard_map/reduce_scatter | solution.py:163
  721.4 25.3 %copy-start.19 = (bf16[768,768]{1,0:T(8,128)(2,1)S(1)}, bf16[768,768]{1,0:T(8,128)(2,1)}, u32[]{:S(2)}) copy-start(bf16[768,768]{1,0:T(8,128)(2,1)} %param.11) | copy-start | bytes 3538948
  745.6 1.2 copy-start.3
  749.4 0.9 copy-start.6
  749.4 258.2 %reduce-scatter.17.cloned.1.call-start = ((), (), s32[]{:S(2)}) async-start(), calls=%async_computation.23 | async-start | bytes 3538944 | tf_op jit(solution)/shard_map/reduce_scatter | solution.py:137
  754.2 0.8 copy-start.10
  754.2 293.9 %reduce-scatter.15.cloned.1.call-start = ((), (), s32[]{:S(2)}) async-start(), calls=%async_computation.22 | async-start | bytes 3538944 | tf_op jit(solution)/shard_map/reduce_scatter | solution.py:134
  768.7 4.5 copy-start.4
  768.7 4.5 copy-start.18
  775.7 191.2 %copy-start.11 = (bf16[32,768]{1,0:T(8,128)(2,1)S(1)}, bf16[32,768]{1,0:T(8,128)(2,1)}, u32[]{:S(2)}) copy-start(bf16[32,768]{1,0:T(8,128)(2,1)} %all_to_all.78) | copy-start | bytes 147460
  (3 other events, 1.8 us)
Sparse Core Ops, SparseCore 0:
  10.6 78.7 all-gather.3
  93.8 33.9 reduce-scatter.6
  130.2 25.6 all-gather.5
  160.4 218.2 reduce-scatter.8
  608.3 73.2 all-gather.7
  686.1 33.9 reduce-scatter.10
  749.5 217.2 reduce-scatter.12
  970.0 37.5 reduce-scatter.16
  1010.8 37.3 reduce-scatter.14
